TPU v7x, 512 devices: a whole 4x4x16 slice. The times are simulated.
512 devices in a mesh: filt: 64 (over y, x, z_hi), slab: 8 (over z_lo, core).
Axes of the slice: x: 4, y: 4, z: 16 (z_hi: 4, z_lo: 4; z = z_hi * 4 + z_lo), core: 2. Of those that a mesh axis runs over, the one named last changes fastest.
Arguments:
- activations: bfloat16 [2048, 16, 512], P('filt', 'slab'), may hold values from -6 to 6
- grad_out: bfloat16 [2048, 16, 512], P('filt', 'slab'), may hold values from -6 to 6
- weights: bfloat16 [27, 256, 256], P(None, 'filt'), may hold values from -0.078125 to 0.078125
Outputs:
- out_map: bfloat16 [2048, 16, 512], P('filt', 'slab')
- grad_in: bfloat16 [2048, 16, 512], P('filt', 'slab')
- filter_grad: float32 [27, 256, 256], P(None, 'filt')
All inputs are finite; a program needn't handle non-finite values.
Results may differ from a plain program's by a relative error of at most 0.001.
Values may be sent and summed in bfloat16 or wider, within the bound.
No kernel may reach another device: no remote copies, remote signals or barrier semaphores. Data moves between devices by JAX's collectives and lax.ppermute only.
A program may use at most 64 MiB of HBM per device.

v0:
```python
import math
import jax
import jax.numpy as jnp
from jax import lax
from jax.sharding import Mesh
from jax.sharding import PartitionSpec as P

CH_IN = 256
CH_OUT = 256
GROUPS = 8
ROWS = 8
WIDTH = 64


def from_offset(value, d_rb, d_slab, n_rb, n_slab):
    if d_slab == 0:
        pairs = [(r + d_rb, r) for r in range(n_rb) if 0 <= r + d_rb < n_rb]
        return lax.ppermute(value, "rb", pairs)
    if d_rb == 0:
        pairs = [(s + d_slab, s) for s in range(n_slab) if 0 <= s + d_slab < n_slab]
        return lax.ppermute(value, "slab", pairs)
    pairs = []
    for r in range(n_rb):
        for s in range(n_slab):
            if 0 <= r + d_rb < n_rb and 0 <= s + d_slab < n_slab:
                pairs.append(((r + d_rb) * n_slab + s + d_slab, r * n_slab + s))
    return lax.ppermute(value, ("rb", "slab"), pairs)


def haloed(block):
    n_rb = lax.axis_size("rb")
    n_slab = lax.axis_size("slab")

    def part(d_rb, d_slab):
        piece = block
        if d_slab < 0:
            piece = piece[:, -1:]
        elif d_slab > 0:
            piece = piece[:, :1]
        if d_rb < 0:
            piece = piece[:, :, -1:]
        elif d_rb > 0:
            piece = piece[:, :, :1]
        if d_rb == 0 and d_slab == 0:
            return piece
        return from_offset(piece, d_rb, d_slab, n_rb, n_slab)

    planes = []
    for d_slab in (-1, 0, 1):
        planes.append(jnp.concatenate([part(d_rb, d_slab) for d_rb in (-1, 0, 1)], axis=2))
    return jnp.concatenate(planes, axis=1)


def correlate(image, kernel, lhs_spec):
    return lax.conv_general_dilated(
        image,
        kernel,
        (1, 1, 1),
        ((0, 0), (0, 0), (1, 1)),
        dimension_numbers=(lhs_spec, "OIDHW", "NCDHW"),
        preferred_element_type=jnp.float32,
    )


def per_device(activations, grad_out, weights):
    chan_local = activations.shape[0]
    depth_dev = activations.shape[1]
    n_rb = lax.axis_size("rb")
    depth_all = depth_dev * lax.axis_size("slab")
    height_all = ROWS * n_rb
    both = jnp.concatenate([activations, grad_out], axis=0).reshape(
        2 * chan_local, depth_dev, ROWS, WIDTH
    )
    whole = lax.all_gather(haloed(both), "grp", axis=0, tiled=False)
    whole_in = whole[:, :chan_local].reshape((CH_IN,) + whole.shape[2:])
    whole_grad = whole[:, chan_local:].reshape((CH_OUT,) + whole.shape[2:])
    group_weights = lax.all_gather(weights, "rb", axis=1, tiled=True)
    column_weights = lax.all_to_all(group_weights, "grp", split_axis=2, concat_axis=1, tiled=True)
    out_kernel = jnp.transpose(group_weights, (1, 2, 0)).reshape(chan_local, CH_IN, 3, 3, 3)
    output_sum = correlate(whole_in[None], out_kernel, "NCDHW")
    grad_kernel = grad_out.reshape(chan_local, 1, depth_dev, ROWS, WIDTH)
    filter_terms = correlate(whole_in[:, None], grad_kernel, "NCDHW")
    filter_part = jnp.transpose(filter_terms.reshape(CH_IN, chan_local, 27), (2, 1, 0))
    in_kernel = jnp.transpose(column_weights[::-1], (2, 1, 0)).reshape(chan_local, CH_OUT, 3, 3, 3)
    input_sum = correlate(whole_grad[None], in_kernel, "NCDHW")
    scale_factor = 1.0 / math.sqrt(depth_all * height_all * WIDTH)
    rows_part = lax.psum_scatter(filter_part, "rb", scatter_dimension=1, tiled=True)
    filter_grad = lax.psum(rows_part, "slab") * scale_factor
    out_map = output_sum.astype(jnp.bfloat16).reshape(chan_local, depth_dev, ROWS * WIDTH)
    grad_in = input_sum.astype(jnp.bfloat16).reshape(chan_local, depth_dev, ROWS * WIDTH)
    return (out_map, grad_in, filter_grad)


def solution(mesh):
    n_filt, n_slab = mesh.devices.shape
    grid = Mesh(mesh.devices.reshape(n_filt // GROUPS, GROUPS, n_slab), ("rb", "grp", "slab"))
    act_spec = P(("rb", "grp"), "slab", None)
    w_spec = P(None, ("rb", "grp"), None)
    in_specs = (act_spec, act_spec, w_spec)
    out_specs = (act_spec, act_spec, w_spec)
    return jax.shard_map(
        per_device, mesh=grid, in_specs=in_specs, out_specs=out_specs, check_vma=False
    )
```

profile of v0, /device:TPU:1, one launch (start us, length us, event | category | flops | bytes accessed | tf_op | source)
XLA Modules:
  0.0 521.8 jit_solution(6389303513420632866)
XLA Ops:
  8.6 7.4 %collective-permute-start = (bf16[64,1,1,64]{3,2,0,1:T(2,128)(2,1)S(1)}, bf16[64,1,1,64]{3,2,0,1:T(2,128)(2,1)S(1)}, u32[]{:S(2)}, u32[]{:S(2)}) collective-permute-start(bf16[64,1,1,64]{3,2,0,1:T(2,128)(2,1)S(1)} %get-tuple-element.14), channel_id=1, source_target_pairs={{0,65},{1,66},{2,67},{3,68},{4,69},{5,70},{6,71},{64,129},{65,130}... | collective-permute-start | bytes 24584 | tf_op jit(solution)/shard_map/ppermute | solution.py:27
  16.0 1.3 collective-permute-start.2
  17.3 5.8 %collective-permute-start.5 = (bf16[64,1,1,64]{3,2,0,1:T(2,128)(2,1)S(1)}, bf16[64,1,1,64]{3,2,0,1:T(2,128)(2,1)S(1)}, u32[]{:S(2)}, u32[]{:S(2)}) collective-permute-start(bf16[64,1,1,64]{3,2,0,1:T(2,128)(2,1)S(1)} %get-tuple-element.16), channel_id=1, source_target_pairs={{1,64},{2,65},{3,66},{4,67},{5,68},{6,69},{7,70},{65,128},{66,129}... | collective-permute-start | bytes 24584 | tf_op jit(solution)/shard_map/ppermute | solution.py:27
  23.1 2.8 collective-permute-start.1
  25.9 1.9 collective-permute-start.6
  27.9 4.1 collective-permute-start.3
  32.0 1.3 collective-permute-start.4
  33.3 1.4 collective-permute-start.7
  34.7 7.8 %collective-permute-done.7 = bf16[64,1,1,64]{3,2,0,1:T(2,128)(2,1)S(1)} collective-permute-done((bf16[64,1,1,64]{3,2,0,1:T(2,128)(2,1)S(1)}, bf16[64,1,1,64]{3,2,0,1:T(2,128)(2,1)S(1)}, u32[]{:S(2)}, u32[]{:S(2)}) %collective-permute-start.7) | collective-permute-done | bytes 8224 | tf_op jit(solution)/shard_map/ppermute | solution.py:27
  43.2 1.7 copy.57
  45.0 31.7 %all_gather.11 = bf16[27,32,256]{2,0,1:T(8,128)(2,1)S(1)} all-gather(bf16[27,4,256]{2,0,1:T(8,128)(2,1)S(1)} %copy.62), channel_id=1, replica_groups=mesh['rb'=8,'grp'=8,'slab'=8] {'rb'}, dimensions={1}, use_global_device_ids=true | all-gather | bytes 497664 | tf_op jit(solution)/shard_map/all_gather | solution.py:77
  76.7 3.2 copy.70
  80.0 2.1 reshape.64
  82.1 14.7 %all-to-all-start = ((bf16[8,2,13824]{2,1,0:T(2,128)(2,1)}), bf16[8,2,13824]{2,1,0:T(2,128)(2,1)S(1)}, u32[]{:S(2)}, u32[]{:S(2)}) async-start(bf16[8,2,13824]{2,1,0:T(2,128)(2,1)} %reshape.64), calls=%async_computation | async-start | bytes 884736 | tf_op jit(solution)/shard_map/all_to_all | solution.py:78
  100.7 99.3 %all-to-all-done = bf16[8,2,13824]{2,1,0:T(2,128)(2,1)S(1)} async-done(((bf16[8,2,13824]{2,1,0:T(2,128)(2,1)}), bf16[8,2,13824]{2,1,0:T(2,128)(2,1)S(1)}, u32[]{:S(2)}, u32[]{:S(2)}) %all-to-all-start) | async-done | bytes 442400 | tf_op jit(solution)/shard_map/all_to_all | solution.py:78
  200.0 1.6 reshape.65
  201.6 2.4 copy.89
  204.0 2.8 all_to_all.16
  207.6 81.8 %all-gather.3.cloned.1.call-done = bf16[512,4,10,64]{3,1,2,0:T(4,128)(2,1)} async-done(((bf16[64,4,10,64]{3,1,2,0:T(4,128)(2,1)}), bf16[512,4,10,64]{3,1,2,0:T(4,128)(2,1)}) %all-gather.3.cloned.1.call-update) | async-done | bytes 2621456 | tf_op jit(solution)/shard_map/all_gather | solution.py:74
  289.4 5.9 %fusion.36 = (bf16[8,32,4,10,64]{4,2,3,1,0:T(4,128)(2,1)}, bf16[8,32,4,10,64]{4,2,3,1,0:T(4,128)(2,1)S(1)}) fusion(bf16[8,64,4,10,64]{4,2,3,1,0:T(4,128)(2,1)} %bitcast.65), kind=kLoop, calls=%fused_computation.34 | loop fusion | bytes 5242880 | tf_op jit(solution)/shard_map/slice | solution.py:76
  296.0 2.5 copy.86
  298.4 1.9 pad.clone
  301.8 5.5 %copy.74 = bf16[256,1,4,10,64]{0,1,4,3,2:T(2,128)(2,1)} copy(bf16[256,1,4,10,64]{4,0,3,2,1:T(8,128)(2,1)S(1)} %bitcast.58) | data formatting | bytes 2621440 | tf_op jit(solution)/shard_map/broadcast_in_dim;reshape | solution.py:82
  307.3 18.5 %fusion.40 = f32[256,32,3,3,3]{0,1,4,3,2:T(8,128)} fusion(bf16[256,1,4,10,64]{0,1,4,3,2:T(2,128)(2,1)} %copy.74, bf16[32,1,2,8,64]{0,1,4,3,2:T(2,128)(2,1)S(1)} %copy.75), kind=kOutput, calls=%fused_computation.38 | convolution fusion | flops 448266240 | bytes 2260992 | tf_op jit(solution)/shard_map/conv_general_dilated | solution.py:55
  325.9 4.3 fusion.22
  330.8 2.7 copy.87
  333.5 1.9 pad.2.clone
  336.5 4.3 fusion.25
  340.8 87.6 %all-reduce.6.cloned.1.call-done = f32[27,32,256]{2,1,0:T(8,128)} async-done(((f32[27,32,256]{2,1,0:T(8,128)}), f32[27,32,256]{2,1,0:T(8,128)}) %all-reduce.6.cloned.1.call-update) | async-done | bytes 884752
  428.4 1.6 constant_dynamic-slice_fusion
  432.1 81.4 %all-reduce.4.cloned.1.call-done = f32[27,4,256]{2,1,0:T(4,128)} async-done(((f32[27,4,256]{2,1,0:T(4,128)}), f32[27,4,256]{2,1,0:T(4,128)}) %all-reduce.4.cloned.1.call-update) | async-done | bytes 110608 | tf_op jit(solution)/shard_map/psum | solution.py:88
  513.5 1.6 broadcast_multiply_fusion
  (56 shorter events, 12.1 us)
Async XLA Ops:
  7.2 282.2 %all-gather.3.cloned.1.call-start = ((), (), s32[]{:S(2)}) async-start(), calls=%async_computation.2 | async-start | bytes 5898240 | tf_op jit(solution)/shard_map/all_gather | solution.py:74
  8.6 19.3 %collective-permute-start = (bf16[64,1,1,64]{3,2,0,1:T(2,128)(2,1)S(1)}, bf16[64,1,1,64]{3,2,0,1:T(2,128)(2,1)S(1)}, u32[]{:S(2)}, u32[]{:S(2)}) collective-permute-start(bf16[64,1,1,64]{3,2,0,1:T(2,128)(2,1)S(1)} %get-tuple-element.14), channel_id=1, source_target_pairs={{0,65},{1,66},{2,67},{3,68},{4,69},{5,70},{6,71},{64,129},{65,130}... | collective-permute-start | bytes 24584 | tf_op jit(solution)/shard_map/ppermute | solution.py:27
  16.0 16.0 %collective-permute-start.2 = (bf16[64,1,1,64]{3,2,0,1:T(2,128)(2,1)S(1)}, bf16[64,1,1,64]{3,2,0,1:T(2,128)(2,1)S(1)}, u32[]{:S(2)}, u32[]{:S(2)}) collective-permute-start(bf16[64,1,1,64]{3,2,0,1:T(2,128)(2,1)S(1)} %get-tuple-element.17), channel_id=1, source_target_pairs={{64,1},{65,2},{66,3},{67,4},{68,5},{69,6},{70,7},{128,65},{129,66}... | collective-permute-start | bytes 24584 | tf_op jit(solution)/shard_map/ppermute | solution.py:27
  17.3 16.0 %collective-permute-start.5 = (bf16[64,1,1,64]{3,2,0,1:T(2,128)(2,1)S(1)}, bf16[64,1,1,64]{3,2,0,1:T(2,128)(2,1)S(1)}, u32[]{:S(2)}, u32[]{:S(2)}) collective-permute-start(bf16[64,1,1,64]{3,2,0,1:T(2,128)(2,1)S(1)} %get-tuple-element.16), channel_id=1, source_target_pairs={{1,64},{2,65},{3,66},{4,67},{5,68},{6,69},{7,70},{65,128},{66,129}... | collective-permute-start | bytes 24584 | tf_op jit(solution)/shard_map/ppermute | solution.py:27
  23.1 19.5 %collective-permute-start.1 = (bf16[64,1,8,64]{3,2,0,1:T(8,128)(2,1)S(1)}, bf16[64,1,8,64]{3,2,0,1:T(8,128)(2,1)S(1)}, u32[]{:S(2)}, u32[]{:S(2)}) collective-permute-start(bf16[64,1,8,64]{3,2,0,1:T(8,128)(2,1)S(1)} %get-tuple-element.18), channel_id=1, source_target_pairs={{0,1},{1,2},{2,3},{3,4},{4,5},{5,6},{6,7},{8,9},{9,10},{10,11},{11... | collective-permute-start | bytes 196616 | tf_op jit(solution)/shard_map/ppermute | solution.py:21
  25.9 16.7 %collective-permute-start.6 = (bf16[64,1,8,64]{3,2,0,1:T(8,128)(2,1)S(1)}, bf16[64,1,8,64]{3,2,0,1:T(8,128)(2,1)S(1)}, u32[]{:S(2)}, u32[]{:S(2)}) collective-permute-start(bf16[64,1,8,64]{3,2,0,1:T(8,128)(2,1)S(1)} %get-tuple-element.19), channel_id=1, source_target_pairs={{1,0},{2,1},{3,2},{4,3},{5,4},{6,5},{7,6},{9,8},{10,9},{11,10},{12... | collective-permute-start | bytes 196616 | tf_op jit(solution)/shard_map/ppermute | solution.py:21
  27.9 14.6 %collective-permute-start.3 = (bf16[64,2,1,64]{3,2,0,1:T(2,128)(2,1)S(1)}, bf16[64,2,1,64]{3,2,0,1:T(2,128)(2,1)S(1)}, u32[]{:S(2)}, u32[]{:S(2)}) collective-permute-start(bf16[64,2,1,64]{3,2,0,1:T(2,128)(2,1)S(1)} %get-tuple-element.20), channel_id=1, source_target_pairs={{0,64},{64,128},{128,192},{192,256},{256,320},{320,384},{384,448},... | collective-permute-start | bytes 49160 | tf_op jit(solution)/shard_map/ppermute | solution.py:18
  32.0 10.6 %collective-permute-start.4 = (bf16[64,2,1,64]{3,2,0,1:T(2,128)(2,1)S(1)}, bf16[64,2,1,64]{3,2,0,1:T(2,128)(2,1)S(1)}, u32[]{:S(2)}, u32[]{:S(2)}) collective-permute-start(bf16[64,2,1,64]{3,2,0,1:T(2,128)(2,1)S(1)} %get-tuple-element.21), channel_id=1, source_target_pairs={{64,0},{128,64},{192,128},{256,192},{320,256},{384,320},{448,384},... | collective-permute-start | bytes 49160 | tf_op jit(solution)/shard_map/ppermute | solution.py:18
  33.3 11.6 %copy-start.6 = (bf16[27,4,256]{2,1,0:T(4,128)(2,1)S(1)}, bf16[27,4,256]{2,1,0:T(4,128)(2,1)}, u32[]{:S(2)}) copy-start(bf16[27,4,256]{2,1,0:T(4,128)(2,1)} %param.5) | copy-start | bytes 165892
  33.3 9.2 %collective-permute-start.7 = (bf16[64,1,1,64]{3,2,0,1:T(2,128)(2,1)S(1)}, bf16[64,1,1,64]{3,2,0,1:T(2,128)(2,1)S(1)}, u32[]{:S(2)}, u32[]{:S(2)}) collective-permute-start(bf16[64,1,1,64]{3,2,0,1:T(2,128)(2,1)S(1)} %get-tuple-element.15), channel_id=1, source_target_pairs={{65,0},{66,1},{67,2},{68,3},{69,4},{70,5},{71,6},{129,64},{130,65}... | collective-permute-start | bytes 24584 | tf_op jit(solution)/shard_map/ppermute | solution.py:27
  80.0 17.1 %copy-start.5 = (bf16[32,2,512]{2,1,0:T(2,128)(2,1)S(1)}, bf16[32,2,512]{2,1,0:T(2,128)(2,1)}, u32[]{:S(2)}) copy-start(bf16[32,2,512]{2,1,0:T(2,128)(2,1)} %param.4) | copy-start | bytes 196612
  82.1 117.9 %all-to-all-start = ((bf16[8,2,13824]{2,1,0:T(2,128)(2,1)}), bf16[8,2,13824]{2,1,0:T(2,128)(2,1)S(1)}, u32[]{:S(2)}, u32[]{:S(2)}) async-start(bf16[8,2,13824]{2,1,0:T(2,128)(2,1)} %reshape.64), calls=%async_computation | async-start | bytes 884736 | tf_op jit(solution)/shard_map/all_to_all | solution.py:78
  96.8 331.6 %all-reduce.6.cloned.1.call-start = ((), (), s32[]{:S(2)}) async-start(), calls=%async_computation.3 | async-start | bytes 1769472
  300.6 1.1 copy-start.1
  307.3 18.6 %copy-start.2 = (bf16[256,4,10,1,8,9]{0,4,5,2,1,3:T(8,128)(2,1)S(1)}, bf16[256,4,10,1,8,9]{0,4,5,2,1,3:T(8,128)(2,1)}, u32[]{:S(2)}) copy-start(bf16[256,4,10,1,8,9]{0,4,5,2,1,3:T(8,128)(2,1)} %copy-done.1) | copy-start | bytes 4423684
  307.3 18.6 %copy-start.4 = (bf16[32,256,27]{1,0,2:T(8,128)(2,1)S(1)}, bf16[32,256,27]{1,0,2:T(8,128)(2,1)}, u32[]{:S(2)}) copy-start(bf16[32,256,27]{1,0,2:T(8,128)(2,1)} %copy.63) | copy-start | bytes 1327108
  307.3 18.6 %copy-start.7 = (pred[8,9]{0,1:T(8,128)(4,1)S(1)}, pred[8,9]{0,1:T(8,128)(4,1)}, u32[]{:S(2)}) copy-start(pred[8,9]{0,1:T(8,128)(4,1)} %constant.13) | copy-start | bytes 220
  325.8 187.7 %all-reduce.4.cloned.1.call-start = ((), (), s32[]{:S(2)}) async-start(), calls=%async_computation.1 | async-start | bytes 221184 | tf_op jit(solution)/shard_map/psum | solution.py:88
  325.9 4.3 copy-start
  335.5 1.0 copy-start.3
Sparse Core Ops, SparseCore 0:
  45.1 244.2 all-gather.2
  325.9 102.4 all-reduce.5
  431.9 81.5 all-reduce.3
where the time goes:
time: 527 us; the launch traced here: 522 us
  waiting for transfers between devices  358 us (68%)
  local copies, waits for them, and re-layouts  45.7 us (9%)
  starting transfers between devices  41 us (8%)
  blocking collectives  31.7 us (6%)
  matrix products  27 us (5%)
  between operations  15.1 us (3%)
    all_to_all x1, waiting for transfers between devices, per_device(): lax.all_to_all(group_weights, 'grp', split_axis=2, concat_axis=1, tiled=T...  99.3 us
    unnamed x4, waiting for transfers between devices  87.6 us
    all_gather x1, waiting for transfers between devices, per_device(): whole = lax.all_gather(haloed(both), 'grp', axis=0, tiled=False)  81.8 us
    psum x1, waiting for transfers between devices, per_device(): filter_grad = lax.psum(rows_part, 'slab') * scale_factor  81.4 us
    all_gather x1, blocking collectives, per_device(): group_weights = lax.all_gather(weights, 'rb', axis=1, tiled=True)  31.7 us
    conv_general_dilated x3, matrix products, correlate(): lax.conv_general_dilated(image, kernel, (1, 1, 1), ((0, 0), (0, 0), (1, 1...  27 us
    unnamed x29, local copies, waits for them, and re-layouts  16.9 us
    ppermute x4, starting transfers between devices, from_offset(): return lax.ppermute(value, ('rb', 'slab'), pairs)  15.9 us
  transfers between devices with their start and end apart: 12, of which 5 were waited for; matrix products, arithmetic and copies ran while one was open for 6% of the time, Pallas kernels for 0%

commit v1 on v0

--- a/solution.py
+++ b/solution.py
@@ -74,7 +74,9 @@
     whole = lax.all_gather(haloed(both), "grp", axis=0, tiled=False)
     whole_in = whole[:, :chan_local].reshape((CH_IN,) + whole.shape[2:])
     whole_grad = whole[:, chan_local:].reshape((CH_OUT,) + whole.shape[2:])
-    group_weights = lax.all_gather(weights, "rb", axis=1, tiled=True)
+    group_weights = jnp.concatenate(
+        lax.all_to_all(jnp.stack([weights] * lax.axis_size("rb")), "rb", 0, 0), axis=1
+    )
     column_weights = lax.all_to_all(group_weights, "grp", split_axis=2, concat_axis=1, tiled=True)
     out_kernel = jnp.transpose(group_weights, (1, 2, 0)).reshape(chan_local, CH_IN, 3, 3, 3)
     output_sum = correlate(whole_in[None], out_kernel, "NCDHW")

time: 527 us -> 530 us (level)
  waiting for transfers between devices: 358 us -> 377 us
  blocking collectives: 31.7 us -> 16.8 us
    all_gather x1, waiting for transfers between devices: 81.8 us -> 145 us  [per_device(): whole = lax.all_gather(haloed(both), 'grp', axis=0, tiled=False)]
    all_to_all x1, waiting for transfers between devices: 99.3 us -> 57 us  [per_device(): lax.all_to_all(group_weights, 'grp', split_axis=2, concat_axis=1, tiled=T...]
    all_gather x1 -> x0, blocking collectives: 31.7 us -> none  [per_device(): group_weights = lax.all_gather(weights, 'rb', axis=1, tiled=True)]
    all_to_all x0 -> x1, blocking collectives: none -> 16.8 us  [per_device(): lax.all_to_all(jnp.stack([weights] * lax.axis_size('rb')), 'rb', 0, 0)]
    unnamed x29 -> x26, local copies, waits for them, and re-layouts: 16.9 us -> 16.2 us
  transfers between devices with their start and end apart: 12 -> 12, of which waited for: 5 -> 5; matrix products, arithmetic and copies ran while one was open for 6% -> 5% of each run, Pallas kernels for 0% -> 0%
where the time goes in v1:
time: 530 us; the launch traced here: 525 us
  waiting for transfers between devices  377 us (71%)
  local copies, waits for them, and re-layouts  44.8 us (8%)
  starting transfers between devices  41.2 us (8%)
  matrix products  27.1 us (5%)
  blocking collectives  16.8 us (3%)
  between operations  15.1 us (3%)
    all_gather x1, waiting for transfers between devices, per_device(): whole = lax.all_gather(haloed(both), 'grp', axis=0, tiled=False)  145 us
    unnamed x4, waiting for transfers between devices  86.1 us
    psum x1, waiting for transfers between devices, per_device(): filter_grad = lax.psum(rows_part, 'slab') * scale_factor  81.4 us
    all_to_all x1, waiting for transfers between devices, per_device(): lax.all_to_all(group_weights, 'grp', split_axis=2, concat_axis=1, tiled=T...  57 us
    conv_general_dilated x3, matrix products, correlate(): lax.conv_general_dilated(image, kernel, (1, 1, 1), ((0, 0), (0, 0), (1, 1...  27.1 us
    all_to_all x1, blocking collectives, per_device(): lax.all_to_all(jnp.stack([weights] * lax.axis_size('rb')), 'rb', 0, 0)  16.8 us
    unnamed x26, local copies, waits for them, and re-layouts  16.2 us
    ppermute x4, starting transfers between devices, from_offset(): return lax.ppermute(value, ('rb', 'slab'), pairs)  15.9 us
  transfers between devices with their start and end apart: 12, of which 5 were waited for; matrix products, arithmetic and copies ran while one was open for 5% of the time, Pallas kernels for 0%

profile of v1, /device:TPU:1, one launch (start us, length us, event | category | flops | bytes accessed | tf_op | source)
XLA Modules:
  0.0 525.2 jit_solution(15586441641353088973)
XLA Ops:
  8.6 7.4 %collective-permute-start = (bf16[64,1,1,64]{3,2,0,1:T(2,128)(2,1)S(1)}, bf16[64,1,1,64]{3,2,0,1:T(2,128)(2,1)S(1)}, u32[]{:S(2)}, u32[]{:S(2)}) collective-permute-start(bf16[64,1,1,64]{3,2,0,1:T(2,128)(2,1)S(1)} %get-tuple-element.14), channel_id=1, source_target_pairs={{0,65},{1,66},{2,67},{3,68},{4,69},{5,70},{6,71},{64,129},{65,130}... | collective-permute-start | bytes 24584 | tf_op jit(solution)/shard_map/ppermute | solution.py:27
  16.0 1.3 collective-permute-start.2
  17.3 5.8 %collective-permute-start.5 = (bf16[64,1,1,64]{3,2,0,1:T(2,128)(2,1)S(1)}, bf16[64,1,1,64]{3,2,0,1:T(2,128)(2,1)S(1)}, u32[]{:S(2)}, u32[]{:S(2)}) collective-permute-start(bf16[64,1,1,64]{3,2,0,1:T(2,128)(2,1)S(1)} %get-tuple-element.16), channel_id=1, source_target_pairs={{1,64},{2,65},{3,66},{4,67},{5,68},{6,69},{7,70},{65,128},{66,129}... | collective-permute-start | bytes 24584 | tf_op jit(solution)/shard_map/ppermute | solution.py:27
  23.1 2.8 collective-permute-start.1
  25.9 1.9 collective-permute-start.6
  27.9 4.1 collective-permute-start.3
  32.0 1.3 collective-permute-start.4
  33.3 1.4 collective-permute-start.7
  34.7 7.8 %collective-permute-done.7 = bf16[64,1,1,64]{3,2,0,1:T(2,128)(2,1)S(1)} collective-permute-done((bf16[64,1,1,64]{3,2,0,1:T(2,128)(2,1)S(1)}, bf16[64,1,1,64]{3,2,0,1:T(2,128)(2,1)S(1)}, u32[]{:S(2)}, u32[]{:S(2)}) %collective-permute-start.7) | collective-permute-done | bytes 8224 | tf_op jit(solution)/shard_map/ppermute | solution.py:27
  43.2 1.7 copy.55
  45.1 16.8 %all_to_all.23 = bf16[8,27,4,256]{3,2,1,0:T(4,128)(2,1)S(1)} all-to-all(bf16[8,27,4,256]{3,2,1,0:T(4,128)(2,1)S(1)} %stack.2), channel_id=1, replica_groups=mesh['rb'=8,'grp'=8,'slab'=8] {'rb'}, dimensions={0} | all-to-all | bytes 884736 | tf_op jit(solution)/shard_map/all_to_all | solution.py:78
  62.3 3.0 copy.67
  65.3 2.1 reshape.74
  67.4 14.8 %all-to-all-start.1 = ((bf16[8,2,13824]{2,1,0:T(2,128)(2,1)}), bf16[8,2,13824]{2,1,0:T(2,128)(2,1)S(1)}, u32[]{:S(2)}, u32[]{:S(2)}) async-start(bf16[8,2,13824]{2,1,0:T(2,128)(2,1)} %reshape.74), calls=%async_computation.1 | async-start | bytes 884736 | tf_op jit(solution)/shard_map/all_to_all | solution.py:80
  85.8 57.0 %all-to-all-done.1 = bf16[8,2,13824]{2,1,0:T(2,128)(2,1)S(1)} async-done(((bf16[8,2,13824]{2,1,0:T(2,128)(2,1)}), bf16[8,2,13824]{2,1,0:T(2,128)(2,1)S(1)}, u32[]{:S(2)}, u32[]{:S(2)}) %all-to-all-start.1) | async-done | bytes 442400 | tf_op jit(solution)/shard_map/all_to_all | solution.py:80
  142.7 1.6 reshape.75
  144.3 2.4 copy.86
  146.8 2.8 all_to_all.20
  149.6 144.7 %all-gather.3.cloned.1.call-done = bf16[512,4,10,64]{3,1,2,0:T(4,128)(2,1)} async-done(((bf16[64,4,10,64]{3,1,2,0:T(4,128)(2,1)}), bf16[512,4,10,64]{3,1,2,0:T(4,128)(2,1)}) %all-gather.3.cloned.1.call-update) | async-done | bytes 2621456 | tf_op jit(solution)/shard_map/all_gather | solution.py:74
  294.3 5.9 %fusion.36 = (bf16[8,32,4,10,64]{4,2,3,1,0:T(4,128)(2,1)}, bf16[8,32,4,10,64]{4,2,3,1,0:T(4,128)(2,1)S(1)}) fusion(bf16[8,64,4,10,64]{4,2,3,1,0:T(4,128)(2,1)} %bitcast.67), kind=kLoop, calls=%fused_computation.34 | loop fusion | bytes 5242880 | tf_op jit(solution)/shard_map/slice | solution.py:76
  300.8 2.5 copy.83
  303.3 1.9 pad.clone
  307.4 5.4 %copy.71 = bf16[256,1,4,10,64]{0,1,4,3,2:T(2,128)(2,1)} copy(bf16[256,1,4,10,64]{4,0,3,2,1:T(8,128)(2,1)S(1)} %bitcast.60) | data formatting | bytes 2621440 | tf_op jit(solution)/shard_map/broadcast_in_dim;reshape | solution.py:84
  312.9 18.6 %fusion.40 = f32[256,32,3,3,3]{0,1,4,3,2:T(8,128)} fusion(bf16[256,1,4,10,64]{0,1,4,3,2:T(2,128)(2,1)} %copy.71, bf16[32,1,2,8,64]{0,1,4,3,2:T(2,128)(2,1)} %copy.72), kind=kOutput, calls=%fused_computation.38 | convolution fusion | flops 448266240 | bytes 2260992 | tf_op jit(solution)/shard_map/conv_general_dilated | solution.py:55
  331.6 4.3 fusion.22
  336.6 2.7 copy.84
  339.3 1.9 pad.2.clone
  341.5 4.3 fusion.25
  345.8 86.0 %all-reduce.6.cloned.1.call-done = f32[27,32,256]{2,1,0:T(8,128)} async-done(((f32[27,32,256]{2,1,0:T(8,128)}), f32[27,32,256]{2,1,0:T(8,128)}) %all-reduce.6.cloned.1.call-update) | async-done | bytes 884752
  431.9 1.6 constant_dynamic-slice_fusion
  435.5 81.4 %all-reduce.4.cloned.1.call-done = f32[27,4,256]{2,1,0:T(4,128)} async-done(((f32[27,4,256]{2,1,0:T(4,128)}), f32[27,4,256]{2,1,0:T(4,128)}) %all-reduce.4.cloned.1.call-update) | async-done | bytes 110608 | tf_op jit(solution)/shard_map/psum | solution.py:90
  516.9 1.6 broadcast_multiply_fusion
  (55 shorter events, 11.4 us)
Async XLA Ops:
  7.2 287.1 %all-gather.3.cloned.1.call-start = ((), (), s32[]{:S(2)}) async-start(), calls=%async_computation.3 | async-start | bytes 5898240 | tf_op jit(solution)/shard_map/all_gather | solution.py:74
  8.6 19.3 %collective-permute-start = (bf16[64,1,1,64]{3,2,0,1:T(2,128)(2,1)S(1)}, bf16[64,1,1,64]{3,2,0,1:T(2,128)(2,1)S(1)}, u32[]{:S(2)}, u32[]{:S(2)}) collective-permute-start(bf16[64,1,1,64]{3,2,0,1:T(2,128)(2,1)S(1)} %get-tuple-element.14), channel_id=1, source_target_pairs={{0,65},{1,66},{2,67},{3,68},{4,69},{5,70},{6,71},{64,129},{65,130}... | collective-permute-start | bytes 24584 | tf_op jit(solution)/shard_map/ppermute | solution.py:27
  16.0 16.0 %collective-permute-start.2 = (bf16[64,1,1,64]{3,2,0,1:T(2,128)(2,1)S(1)}, bf16[64,1,1,64]{3,2,0,1:T(2,128)(2,1)S(1)}, u32[]{:S(2)}, u32[]{:S(2)}) collective-permute-start(bf16[64,1,1,64]{3,2,0,1:T(2,128)(2,1)S(1)} %get-tuple-element.17), channel_id=1, source_target_pairs={{64,1},{65,2},{66,3},{67,4},{68,5},{69,6},{70,7},{128,65},{129,66}... | collective-permute-start | bytes 24584 | tf_op jit(solution)/shard_map/ppermute | solution.py:27
  17.3 16.0 %collective-permute-start.5 = (bf16[64,1,1,64]{3,2,0,1:T(2,128)(2,1)S(1)}, bf16[64,1,1,64]{3,2,0,1:T(2,128)(2,1)S(1)}, u32[]{:S(2)}, u32[]{:S(2)}) collective-permute-start(bf16[64,1,1,64]{3,2,0,1:T(2,128)(2,1)S(1)} %get-tuple-element.16), channel_id=1, source_target_pairs={{1,64},{2,65},{3,66},{4,67},{5,68},{6,69},{7,70},{65,128},{66,129}... | collective-permute-start | bytes 24584 | tf_op jit(solution)/shard_map/ppermute | solution.py:27
  23.1 19.5 %collective-permute-start.1 = (bf16[64,1,8,64]{3,2,0,1:T(8,128)(2,1)S(1)}, bf16[64,1,8,64]{3,2,0,1:T(8,128)(2,1)S(1)}, u32[]{:S(2)}, u32[]{:S(2)}) collective-permute-start(bf16[64,1,8,64]{3,2,0,1:T(8,128)(2,1)S(1)} %get-tuple-element.18), channel_id=1, source_target_pairs={{0,1},{1,2},{2,3},{3,4},{4,5},{5,6},{6,7},{8,9},{9,10},{10,11},{11... | collective-permute-start | bytes 196616 | tf_op jit(solution)/shard_map/ppermute | solution.py:21
  25.9 16.7 %collective-permute-start.6 = (bf16[64,1,8,64]{3,2,0,1:T(8,128)(2,1)S(1)}, bf16[64,1,8,64]{3,2,0,1:T(8,128)(2,1)S(1)}, u32[]{:S(2)}, u32[]{:S(2)}) collective-permute-start(bf16[64,1,8,64]{3,2,0,1:T(8,128)(2,1)S(1)} %get-tuple-element.19), channel_id=1, source_target_pairs={{1,0},{2,1},{3,2},{4,3},{5,4},{6,5},{7,6},{9,8},{10,9},{11,10},{12... | collective-permute-start | bytes 196616 | tf_op jit(solution)/shard_map/ppermute | solution.py:21
  27.9 14.6 %collective-permute-start.3 = (bf16[64,2,1,64]{3,2,0,1:T(2,128)(2,1)S(1)}, bf16[64,2,1,64]{3,2,0,1:T(2,128)(2,1)S(1)}, u32[]{:S(2)}, u32[]{:S(2)}) collective-permute-start(bf16[64,2,1,64]{3,2,0,1:T(2,128)(2,1)S(1)} %get-tuple-element.20), channel_id=1, source_target_pairs={{0,64},{64,128},{128,192},{192,256},{256,320},{320,384},{384,448},... | collective-permute-start | bytes 49160 | tf_op jit(solution)/shard_map/ppermute | solution.py:18
  32.0 10.6 %collective-permute-start.4 = (bf16[64,2,1,64]{3,2,0,1:T(2,128)(2,1)S(1)}, bf16[64,2,1,64]{3,2,0,1:T(2,128)(2,1)S(1)}, u32[]{:S(2)}, u32[]{:S(2)}) collective-permute-start(bf16[64,2,1,64]{3,2,0,1:T(2,128)(2,1)S(1)} %get-tuple-element.21), channel_id=1, source_target_pairs={{64,0},{128,64},{192,128},{256,192},{320,256},{384,320},{448,384},... | collective-permute-start | bytes 49160 | tf_op jit(solution)/shard_map/ppermute | solution.py:18
  33.3 11.7 %copy-start.5 = (bf16[27,4,256]{2,1,0:T(4,128)(2,1)S(1)}, bf16[27,4,256]{2,1,0:T(4,128)(2,1)}, u32[]{:S(2)}) copy-start(bf16[27,4,256]{2,1,0:T(4,128)(2,1)} %param.5) | copy-start | bytes 165892
  33.3 9.2 %collective-permute-start.7 = (bf16[64,1,1,64]{3,2,0,1:T(2,128)(2,1)S(1)}, bf16[64,1,1,64]{3,2,0,1:T(2,128)(2,1)S(1)}, u32[]{:S(2)}, u32[]{:S(2)}) collective-permute-start(bf16[64,1,1,64]{3,2,0,1:T(2,128)(2,1)S(1)} %get-tuple-element.15), channel_id=1, source_target_pairs={{65,0},{66,1},{67,2},{68,3},{69,4},{70,5},{71,6},{129,64},{130,65}... | collective-permute-start | bytes 24584 | tf_op jit(solution)/shard_map/ppermute | solution.py:27
  65.3 17.3 %copy-start.4 = (bf16[32,2,512]{2,1,0:T(2,128)(2,1)S(1)}, bf16[32,2,512]{2,1,0:T(2,128)(2,1)}, u32[]{:S(2)}) copy-start(bf16[32,2,512]{2,1,0:T(2,128)(2,1)} %param.4) | copy-start | bytes 196612
  67.4 75.4 %all-to-all-start.1 = ((bf16[8,2,13824]{2,1,0:T(2,128)(2,1)}), bf16[8,2,13824]{2,1,0:T(2,128)(2,1)S(1)}, u32[]{:S(2)}, u32[]{:S(2)}) async-start(bf16[8,2,13824]{2,1,0:T(2,128)(2,1)} %reshape.74), calls=%async_computation.1 | async-start | bytes 884736 | tf_op jit(solution)/shard_map/all_to_all | solution.py:80
  82.2 349.6 %all-reduce.6.cloned.1.call-start = ((), (), s32[]{:S(2)}) async-start(), calls=%async_computation.4 | async-start | bytes 1769472
  305.5 1.1 copy-start.1
  312.9 18.7 %copy-start.2 = (bf16[256,4,10,1,8,9]{0,4,5,2,1,3:T(8,128)(2,1)S(1)}, bf16[256,4,10,1,8,9]{0,4,5,2,1,3:T(8,128)(2,1)}, u32[]{:S(2)}) copy-start(bf16[256,4,10,1,8,9]{0,4,5,2,1,3:T(8,128)(2,1)} %copy-done.1) | copy-start | bytes 4423684
  312.9 18.7 %copy-start.3 = (bf16[256,4,10,1,7,2]{0,4,5,2,1,3:T(8,128)(2,1)S(1)}, bf16[256,4,10,1,7,2]{0,4,5,2,1,3:T(8,128)(2,1)}, u32[]{:S(2)}) copy-start(bf16[256,4,10,1,7,2]{0,4,5,2,1,3:T(8,128)(2,1)} %slice.61) | copy-start | bytes 860164
  312.9 18.7 %copy-start.6 = (pred[8,9]{0,1:T(8,128)(4,1)S(1)}, pred[8,9]{0,1:T(8,128)(4,1)}, u32[]{:S(2)}) copy-start(pred[8,9]{0,1:T(8,128)(4,1)} %constant.13) | copy-start | bytes 220
  331.5 185.4 %all-reduce.4.cloned.1.call-start = ((), (), s32[]{:S(2)}) async-start(), calls=%async_computation.2 | async-start | bytes 221184 | tf_op jit(solution)/shard_map/psum | solution.py:90
  331.6 4.3 copy-start
Sparse Core Ops, SparseCore 0:
  45.1 249.1 all-gather.2
  331.6 100.1 all-reduce.5
  435.4 81.5 all-reduce.3
